TPU v7x, 32 devices: a whole 2x2x4 slice. The times are simulated.
32 devices in a mesh: dp: 4 (over y, x), expert: 8 (over z, core).
Axes of the slice: x: 2, y: 2, z: 4, core: 2. Of those that a mesh axis runs over, the one named last changes fastest.
Arguments:
- context: bfloat16 [8, 4, 128, 1536], P('expert', None, None, 'dp'), may hold values from -0.29882812 to 0.29882812
- w_proj: bfloat16 [1536, 1536], P('dp'), may hold values from -0.15625 to 0.15625
- residual: bfloat16 [4096, 1536], P(('dp', 'expert')), may hold values from -0.29882812 to 0.29882812
- gain_first: float32 [1536], replicated, may hold values from 0.25 to 1.75
- gain_next: float32 [1536], replicated, may hold values from 0.25 to 1.75
- w_router: bfloat16 [1536, 40], replicated, may hold values from -0.15625 to 0.15625
- expert_ids: int32 [4096, 8], P(('dp', 'expert')), may hold values from 0 to 39, all different within a row
- replica_pick: int32 [4096, 8], P(('dp', 'expert')), may hold values from 0 to 5039
- slot_expert: int32 [48], replicated, may hold values from 0 to 39, as said below
- cap_blocks: int32 [48], replicated, may hold values from 1 to 4
- w_in: bfloat16 [48, 1536, 1024], P('expert', 'dp'), as said below
- w_out: bfloat16 [48, 512, 1536], P('expert', 'dp'), as said below
Outputs:
- residual_out: bfloat16 [4096, 1536], P(('dp', 'expert'))
- next_normed: bfloat16 [4096, 1536], P(('dp', 'expert'))
Inputs may be any that keep to these rules, and one draw needn't show every extreme that they name: `slot_expert`: every expert is held by at least one slot; slot s lies on index s // 6 of the expert axis. `w_in`: two slots that hold the same expert have equal weights. `w_out`: two slots that hold the same expert have equal weights.
All inputs are finite; a program needn't handle non-finite values.
Results may differ from a plain program's by a relative error of at most 0.01.
Values may be sent and summed in bfloat16 or wider, within the bound.
No kernel may reach another device: no remote copies, remote signals or barrier semaphores. Data moves between devices by JAX's collectives and lax.ppermute only.
A program may use at most 128 MiB of HBM per device.

v0:
```python
import math
import jax
import jax.numpy as jnp
from jax import lax
from jax.sharding import PartitionSpec as P

CAP_UNIT = 8
CAP_MOST = 32


def rms_scale(values, gain):
    widened = values.astype(jnp.float32)
    return widened * lax.rsqrt(jnp.mean(widened * widened, axis=-1, keepdims=True) + 1e-06) * gain


def route_rows(normed, w_router, expert_ids, replica_pick, slot_expert, cap_blocks, cap_unit):
    blocks, row_count, topk_all = expert_ids.shape
    experts_all = w_router.shape[1]
    slots_all = slot_expert.shape[0]
    logits = jnp.dot(normed, w_router, preferred_element_type=jnp.float32)
    logits = logits.reshape(blocks, row_count, experts_all)
    expert_axis = jnp.arange(experts_all)
    one_hot = expert_ids[..., None] == expert_axis
    chosen = jnp.sum(jnp.where(one_hot, logits[:, :, None, :], jnp.float32(0.0)), axis=-1)
    raised = jnp.exp(chosen)
    gates = raised / jnp.sum(raised, axis=-1, keepdims=True)
    holder = (slot_expert[None, :] == expert_axis[:, None]).astype(jnp.int32)
    rep_count = jnp.sum(holder, axis=1)
    earlier = jnp.cumsum(holder, axis=1) - holder
    slot_rank = jnp.sum(earlier * holder, axis=0)
    count_of = jnp.sum(jnp.where(one_hot, rep_count, 0), axis=-1)
    replica = replica_pick % count_of
    slot_axis = jnp.arange(slots_all)
    matched = (slot_expert == expert_ids[..., None]) & (slot_rank == replica[..., None])
    target_slot = jnp.sum(jnp.where(matched, slot_axis, 0), axis=-1)
    flat_count = row_count * topk_all
    selected = matched.reshape(blocks, flat_count, slots_all)
    flat_axis = lax.optimization_barrier(jnp.arange(flat_count))
    lower = (flat_axis[:, None] > flat_axis[None, :]).astype(jnp.bfloat16)
    before = jnp.einsum(
        "ij,bjs->bis", lower, selected.astype(jnp.bfloat16), preferred_element_type=jnp.float32
    )
    position = (
        jnp.sum(jnp.where(selected, before, jnp.float32(0.0)), axis=-1)
        .astype(jnp.int32)
        .reshape(blocks, row_count, topk_all)
    )
    capacity = (
        jnp.sum(jnp.where(target_slot[..., None] == slot_axis, cap_blocks, 0), axis=-1) * cap_unit
    )
    retained = position < capacity
    return (gates, target_slot, position, retained)


def unit_plan(slot_local, n_dp, hidden_units):
    full = slot_local // n_dp
    rest = slot_local - full * n_dp
    chunks = n_dp // math.gcd(rest, n_dp) if rest else 1
    halves = rest * chunks // n_dp
    chunk_width = hidden_units // chunks
    owned_full = [[o * full + j for j in range(full)] for o in range(n_dp)]
    owned_part = [
        [
            (full * n_dp + (o * halves + i) // chunks, (o * halves + i) % chunks)
            for i in range(halves)
        ]
        for o in range(n_dp)
    ]
    return (full, halves, chunks, chunk_width, owned_full, owned_part)


def on_device(
    context,
    w_proj,
    residual,
    gain_first,
    gain_next,
    w_router,
    expert_ids,
    replica_pick,
    slot_expert,
    cap_blocks,
    w_in,
    w_out,
):
    tok_rows, model_width = residual.shape
    topk_all = expert_ids.shape[1]
    slot_local, d_local, _ = w_in.shape
    hidden_units = w_in.shape[2] // 2
    ff_local = w_out.shape[1]
    n_dp = lax.axis_size("dp")
    n_exp = lax.axis_size("expert")
    dp_at = lax.axis_index("dp")
    exp_at = lax.axis_index("expert")
    full, halves, chunks, chunk_width, owned_full, owned_part = unit_plan(
        slot_local, n_dp, hidden_units
    )
    sources_per_chunk = chunk_width // ff_local
    lane_width = 2 * chunk_width if ff_local * model_width % (2 * chunk_width) == 0 else 128

    def as_rows(piece):
        return piece.reshape(-1, lane_width)

    weight_parts = []
    for o in range(n_dp):
        pieces = []
        for s in owned_full[o]:
            pieces += [as_rows(w_in[s]), as_rows(w_out[s])]
        for s, c in owned_part[o]:
            lo = c * chunk_width
            pieces += [
                as_rows(w_in[s, :, lo : lo + chunk_width]),
                as_rows(w_in[s, :, hidden_units + lo : hidden_units + lo + chunk_width]),
                as_rows(w_out[s]),
            ]
        weight_parts.append(jnp.concatenate(pieces, axis=0))
    weight_recv = lax.all_to_all(jnp.stack(weight_parts), "dp", 0, 0, tiled=True)
    offset = 0

    def take(shape):
        nonlocal offset
        count = math.prod(shape) // lane_width
        piece = weight_recv[:, offset : offset + count].reshape((n_dp,) + shape)
        offset += count
        return piece

    full_in, full_out, part_in, part_out = ([], [], [], [])
    for _ in range(full):
        full_in.append(take((d_local, 2 * hidden_units)).reshape(n_dp * d_local, 2 * hidden_units))
        full_out.append(take((ff_local, model_width)).reshape(n_dp * ff_local, model_width))
    for _ in range(halves):
        gate_in = take((d_local, chunk_width))
        up_in = take((d_local, chunk_width))
        part_in.append(
            jnp.concatenate([gate_in, up_in], axis=-1).reshape(n_dp * d_local, 2 * chunk_width)
        )
        part_out.append(take((ff_local, model_width)))
    ids_all = lax.all_gather(
        jnp.concatenate([expert_ids, replica_pick], axis=1), "expert", axis=0, tiled=True
    ).reshape(n_exp, tok_rows, 2 * topk_all)
    flat_context = context.reshape(-1, context.shape[3])
    attended = lax.psum_scatter(
        jnp.dot(flat_context, w_proj, preferred_element_type=jnp.float32).astype(jnp.bfloat16),
        "dp",
        scatter_dimension=0,
        tiled=True,
    )
    hidden_state = (residual.astype(jnp.float32) + attended.astype(jnp.float32)).astype(
        jnp.bfloat16
    )
    normed = rms_scale(hidden_state, gain_first).astype(jnp.bfloat16)
    normed_all = lax.all_gather(normed, "expert", axis=0, tiled=True)
    gates, target_slot, position, retained = route_rows(
        normed_all,
        w_router,
        ids_all[:, :, :topk_all],
        ids_all[:, :, topk_all:],
        slot_expert,
        cap_blocks,
        CAP_UNIT,
    )
    here = retained & (target_slot // slot_local == exp_at)
    local = jnp.where(here, target_slot % slot_local * CAP_MOST + position, -1)
    hit = local[..., None] == jnp.arange(slot_local * CAP_MOST)
    pick = jnp.any(hit, axis=2).astype(jnp.bfloat16)
    weight = jnp.sum(jnp.where(hit, gates[..., None], jnp.float32(0.0)), axis=2)
    slot_in = jnp.einsum(
        "btr,btd->brd",
        pick,
        normed_all.reshape(n_exp, tok_rows, model_width),
        preferred_element_type=jnp.float32,
    ).astype(jnp.bfloat16)
    slot_in = slot_in.reshape(n_exp, slot_local, CAP_MOST, model_width)
    x_parts = []
    for o in range(n_dp):
        x_parts.append(
            jnp.stack(
                [slot_in[:, s] for s in owned_full[o]] + [slot_in[:, s] for s, _ in owned_part[o]]
            )
        )
    x_recv = lax.all_to_all(jnp.stack(x_parts), "dp", 0, 0, tiled=True)
    unit_rows = n_dp * n_exp * CAP_MOST

    def expert_rows(rows, w_up, w_down, width):
        gate_up = jnp.dot(rows, w_up, preferred_element_type=jnp.float32)
        activated = (jax.nn.silu(gate_up[:, :width]) * gate_up[:, width:]).astype(jnp.bfloat16)
        return jnp.dot(activated, w_down, preferred_element_type=jnp.float32).astype(jnp.bfloat16)

    outs = []
    for j in range(full):
        rows = x_recv[:, j].reshape(unit_rows, model_width)
        outs.append(expert_rows(rows, full_in[j], full_out[j], hidden_units))
    for i in range(halves):
        rows = x_recv[:, full + i].reshape(unit_rows, model_width)
        chunk_at = (dp_at * halves + i) % chunks
        w_down = lax.dynamic_slice_in_dim(
            part_out[i], chunk_at * sources_per_chunk, sources_per_chunk, axis=0
        ).reshape(chunk_width, model_width)
        outs.append(expert_rows(rows, part_in[i], w_down, chunk_width))
    y_send = (
        jnp.stack(outs)
        .reshape(full + halves, n_dp, n_exp, CAP_MOST, model_width)
        .transpose(1, 0, 2, 3, 4)
    )
    y_recv = lax.all_to_all(y_send, "dp", 0, 0, tiled=True)
    slot_out = [None] * slot_local
    for o in range(n_dp):
        for j, s in enumerate(owned_full[o]):
            slot_out[s] = y_recv[o, j]
        for i, (s, _) in enumerate(owned_part[o]):
            part = y_recv[o, full + i].astype(jnp.float32)
            slot_out[s] = part if slot_out[s] is None else slot_out[s] + part
    slot_out = [part.astype(jnp.bfloat16) for part in slot_out]
    expert_out = (
        jnp.stack(slot_out, axis=1)
        .reshape(n_exp, slot_local * CAP_MOST, model_width)
        .astype(jnp.bfloat16)
    )
    weight_hi = weight.astype(jnp.bfloat16)
    weight_lo = (weight - weight_hi.astype(jnp.float32)).astype(jnp.bfloat16)
    partial = jnp.einsum(
        "btr,brd->btd", weight_hi, expert_out, preferred_element_type=jnp.float32
    ) + jnp.einsum("btr,brd->btd", weight_lo, expert_out, preferred_element_type=jnp.float32)
    combined = lax.psum_scatter(
        partial.reshape(n_exp * tok_rows, model_width), "expert", scatter_dimension=0, tiled=True
    )
    residual_out = (hidden_state.astype(jnp.float32) + combined.astype(jnp.float32)).astype(
        jnp.bfloat16
    )
    next_normed = rms_scale(residual_out, gain_next).astype(jnp.bfloat16)
    return (residual_out, next_normed)


def solution(mesh):
    placed = (
        P("expert", None, None, "dp"),
        P("dp", None),
        P(("dp", "expert"), None),
        P(),
        P(),
        P(),
        P(("dp", "expert"), None),
        P(("dp", "expert"), None),
        P(),
        P(),
        P("expert", "dp", None),
        P("expert", "dp", None),
    )
    return jax.shard_map(
        on_device,
        mesh=mesh,
        in_specs=placed,
        out_specs=(P(("dp", "expert"), None), P(("dp", "expert"), None)),
        check_vma=False,
    )
```

profile of v0, /device:TPU:0, one launch (start us, length us, event | category | flops | bytes accessed | tf_op | source)
XLA Modules:
  0.0 409.4 jit_solution(10336887826829885044)
XLA Ops:
  8.4 3.1 convolution_convert_fusion.3
  11.7 2.3 fusion.60
  14.0 1.8 reshape_squeeze.66
  15.8 1.7 reshape_squeeze.75
  24.4 1.9 reshape_squeeze.73
  26.3 2.0 reshape_squeeze.69
  31.1 2.2 fusion.61
  42.9 2.7 reduce-scatter.3.cloned.1.call-done
  46.9 1.9 fusion.26
  48.8 1.7 constant_dynamic-update-slice_fusion.12
  54.2 6.1 %pad_maximum_fusion = bf16[4,1920,512]{2,1,0:T(8,128)(2,1)} fusion(bf16[1,1920,512]{2,1,0:T(8,128)(2,1)} %bitcast.19, bf16[1,1920,512]{2,1,0:T(8,128)(2,1)} %bitcast.18, bf16[1,1920,512]{2,1,0:T(8,128)(2,1)S(1)} %bitcast.110, bf16[1,1920,512]{2,1,0:T(8,128)(2,1)S(1)} %bitcast.111), kind=kLoop, calls=%fused_computation | loop fusion | flops 11796480 | bytes 15728640 | tf_op jit(solution)/shard_map/stack | solution.py:117
  60.3 5.7 %all-to-all-start.1 = ((bf16[4,1920,512]{2,1,0:T(8,128)(2,1)}), bf16[4,1920,512]{2,1,0:T(8,128)(2,1)}, u32[]{:S(2)}, u32[]{:S(2)}) async-start(bf16[4,1920,512]{2,1,0:T(8,128)(2,1)} %pad_maximum_fusion), calls=%async_computation.2 | async-start | bytes 15728640 | tf_op jit(solution)/shard_map/all_to_all | solution.py:117
  66.0 14.7 %all_gather.6 = s32[1024,16]{0,1:T(8,128)S(1)} all-gather(s32[128,16]{0,1:T(8,128)S(1)} %pad_add_fusion), channel_id=1, replica_groups=mesh['dp'=4,'expert'=8] {'expert'}, dimensions={0}, use_global_device_ids=true | all-gather | bytes 73728 | tf_op jit(solution)/shard_map/all_gather | solution.py:138
  87.7 3.3 convolution_convert_fusion
  92.0 3.5 pad_maximum_fusion.1
  95.5 57.2 %all-to-all-done.1 = bf16[4,1920,512]{2,1,0:T(8,128)(2,1)} async-done(((bf16[4,1920,512]{2,1,0:T(8,128)(2,1)}), bf16[4,1920,512]{2,1,0:T(8,128)(2,1)}, u32[]{:S(2)}, u32[]{:S(2)}) %all-to-all-start.1) | async-done | bytes 7864352 | tf_op jit(solution)/shard_map/all_to_all | solution.py:117
  152.8 5.5 %all-to-all-start = ((bf16[4,2,8,32,1536]{4,3,2,1,0:T(8,128)(2,1)}), bf16[4,2,8,32,1536]{4,3,2,1,0:T(8,128)(2,1)}, u32[]{:S(2)}, u32[]{:S(2)}) async-start(bf16[4,2,8,32,1536]{4,3,2,1,0:T(8,128)(2,1)} %pad_maximum_fusion.1), calls=%async_computation.1 | async-start | bytes 12582912 | tf_op jit(solution)/shard_map/all_to_all | solution.py:181
  162.2 3.4 fusion.57
  165.6 3.7 reshape_reshape.7
  169.3 3.8 slice.193
  173.1 5.7 %reshape_reshape.6 = bf16[1536,1024]{1,0:T(8,128)(2,1)} reshape(bf16[4,768,512]{2,1,0:T(8,128)(2,1)} %slice.193) | data formatting | bytes 6291456 | tf_op jit(solution)/shard_map/reshape;reshape | solution.py:129
  181.6 45.9 %all-to-all-done = bf16[4,2,8,32,1536]{4,3,2,1,0:T(8,128)(2,1)} async-done(((bf16[4,2,8,32,1536]{4,3,2,1,0:T(8,128)(2,1)}), bf16[4,2,8,32,1536]{4,3,2,1,0:T(8,128)(2,1)}, u32[]{:S(2)}, u32[]{:S(2)}) %all-to-all-start) | async-done | bytes 6291488 | tf_op jit(solution)/shard_map/all_to_all | solution.py:181
  227.5 3.4 fusion.59
  231.2 3.4 fusion.64
  234.7 1.8 convolution_convert_fusion.2
  236.5 1.8 fusion.11
  239.3 3.2 maximum_bitcast_fusion
  242.5 5.4 %all-to-all-start.2 = ((bf16[4,2,8,32,1536]{4,3,2,1,0:T(8,128)(2,1)}), bf16[4,2,8,32,1536]{4,3,2,1,0:T(8,128)(2,1)}, u32[]{:S(2)}, u32[]{:S(2)}) async-start(bf16[4,2,8,32,1536]{4,3,2,1,0:T(8,128)(2,1)} %maximum_bitcast_fusion), calls=%async_computation.3 | async-start | bytes 12582912 | tf_op jit(solution)/shard_map/all_to_all | solution.py:205
  248.2 2.9 convolution_bitcast_fusion
  252.6 64.7 %all-to-all-done.2 = bf16[4,2,8,32,1536]{4,3,2,1,0:T(8,128)(2,1)} async-done(((bf16[4,2,8,32,1536]{4,3,2,1,0:T(8,128)(2,1)}), bf16[4,2,8,32,1536]{4,3,2,1,0:T(8,128)(2,1)}, u32[]{:S(2)}, u32[]{:S(2)}) %all-to-all-start.2) | async-done | bytes 6291488 | tf_op jit(solution)/shard_map/all_to_all | solution.py:205
  326.8 3.7 convolution_add_fusion
  330.6 69.9 %reduce-scatter.5.cloned.1.call-done = f32[128,1536]{1,0:T(8,128)} async-done(((f32[1024,1536]{1,0:T(8,128)}), f32[128,1536]{1,0:T(8,128)}) %reduce-scatter.5.cloned.1.call-update) | async-done | bytes 786448 | tf_op jit(solution)/shard_map/reduce_scatter | solution.py:224
  (149 shorter events, 54.8 us)
Async XLA Ops:
  7.2 38.5 %reduce-scatter.3.cloned.1.call-start = ((), (), s32[]{:S(2)}) async-start(), calls=%async_computation.5 | async-start | bytes 1966080 | tf_op jit(solution)/shard_map/reduce_scatter | solution.py:142
  11.6 76.1 %all-gather.2.cloned.1.call-start = ((), (), s32[]{:S(2)}) async-start(), calls=%async_computation.6 | async-start | bytes 3538944 | tf_op jit(solution)/shard_map/all_gather | solution.py:152
  14.0 8.0 %copy-start.8 = (bf16[6,128,1536]{2,1,0:T(8,128)(2,1)S(1)}, bf16[6,128,1536]{2,1,0:T(8,128)(2,1)}, u32[]{:S(2)}) copy-start(bf16[6,128,1536]{2,1,0:T(8,128)(2,1)} %param.23) | copy-start | bytes 7077892
  23.1 5.1 %copy-start.13 = (bf16[1,128,1536]{2,1,0:T(8,128)(2,1)S(1)}, bf16[1,128,1536]{2,1,0:T(8,128)(2,1)}, u32[]{:S(2)}) copy-start(bf16[1,128,1536]{2,1,0:T(8,128)(2,1)} %get-tuple-element.33) | copy-start | bytes 1179652
  36.7 2.5 copy-start.12
  37.9 2.5 copy-start.10
  39.2 1.9 copy-start.6
  39.4 2.7 copy-start.11
  40.3 5.3 %copy-start.2 = (bf16[128,1536]{1,0:T(8,128)(2,1)S(1)}, bf16[128,1536]{1,0:T(8,128)(2,1)}, u32[]{:S(2)}) copy-start(bf16[128,1536]{1,0:T(8,128)(2,1)} %param.14) | copy-start | bytes 1179652
  40.4 6.5 %copy-start.26 = (f32[1536]{0:T(1024)S(1)}, f32[1536]{0:T(1024)}, u32[]{:S(2)}) copy-start(f32[1536]{0:T(1024)} %param.15) | copy-start | bytes 18436
  42.1 10.1 %copy-start.5 = (bf16[768,512]{1,0:T(8,128)(2,1)S(1)}, bf16[768,512]{1,0:T(8,128)(2,1)}, u32[]{:S(2)}) copy-start(bf16[768,512]{1,0:T(8,128)(2,1)} %reshape_squeeze.63) | copy-start | bytes 2359300
  48.8 3.5 copy-start.19
  48.8 3.5 copy-start.23
  48.8 3.5 copy-start.24
  50.5 2.6 copy-start.21
  50.5 2.6 copy-start.22
  52.2 1.9 copy-start.14
  60.3 5.7 %copy-start.29 = (s32[128,8]{0,1:T(8,128)S(1)}, s32[128,8]{0,1:T(8,128)}, u32[]{:S(2)}) copy-start(s32[128,8]{0,1:T(8,128)} %param.19) | copy-start | bytes 12292
  60.3 5.7 %copy-start.30 = (s32[128,8]{0,1:T(8,128)S(1)}, s32[128,8]{0,1:T(8,128)}, u32[]{:S(2)}) copy-start(s32[128,8]{0,1:T(8,128)} %param.18) | copy-start | bytes 12292
  60.3 20.7 %copy-start.28 = (s32[48]{0:T(128)S(1)}, s32[48]{0:T(128)}, u32[]{:S(2)}) copy-start(s32[48]{0:T(128)} %param.20) | copy-start | bytes 580
  60.3 92.5 %all-to-all-start.1 = ((bf16[4,1920,512]{2,1,0:T(8,128)(2,1)}), bf16[4,1920,512]{2,1,0:T(8,128)(2,1)}, u32[]{:S(2)}, u32[]{:S(2)}) async-start(bf16[4,1920,512]{2,1,0:T(8,128)(2,1)} %pad_maximum_fusion), calls=%async_computation.2 | async-start | bytes 15728640 | tf_op jit(solution)/shard_map/all_to_all | solution.py:117
  82.9 2.7 copy-start.31
  152.8 74.7 %all-to-all-start = ((bf16[4,2,8,32,1536]{4,3,2,1,0:T(8,128)(2,1)}), bf16[4,2,8,32,1536]{4,3,2,1,0:T(8,128)(2,1)}, u32[]{:S(2)}, u32[]{:S(2)}) async-start(bf16[4,2,8,32,1536]{4,3,2,1,0:T(8,128)(2,1)} %pad_maximum_fusion.1), calls=%async_computation.1 | async-start | bytes 12582912 | tf_op jit(solution)/shard_map/all_to_all | solution.py:181
  227.5 3.7 copy-start.4
  231.2 3.4 copy-start.9
  234.6 1.9 copy-start.17
  242.5 5.7 %copy-start.25 = (bf16[1536,40]{0,1:T(8,128)(2,1)S(1)}, bf16[1536,40]{0,1:T(8,128)(2,1)}, u32[]{:S(2)}) copy-start(bf16[1536,40]{0,1:T(8,128)(2,1)} %param.17) | copy-start | bytes 368644
  242.5 74.8 %all-to-all-start.2 = ((bf16[4,2,8,32,1536]{4,3,2,1,0:T(8,128)(2,1)}), bf16[4,2,8,32,1536]{4,3,2,1,0:T(8,128)(2,1)}, u32[]{:S(2)}, u32[]{:S(2)}) async-start(bf16[4,2,8,32,1536]{4,3,2,1,0:T(8,128)(2,1)} %maximum_bitcast_fusion), calls=%async_computation.3 | async-start | bytes 12582912 | tf_op jit(solution)/shard_map/all_to_all | solution.py:205
  247.9 152.6 %reduce-scatter.5.cloned.1.call-start = ((), (), s32[]{:S(2)}) async-start(), calls=%async_computation.7 | async-start | bytes 7077888 | tf_op jit(solution)/shard_map/reduce_scatter | solution.py:224
  330.5 70.0 %copy-start.3 = (bf16[128,1536]{1,0:T(8,128)(2,1)S(1)}, bf16[128,1536]{1,0:T(8,128)(2,1)}, u32[]{:S(2)}) copy-start(bf16[128,1536]{1,0:T(8,128)(2,1)} %reduce-scatter.3.cloned.1.call-done) | copy-start | bytes 1179652
  330.6 71.3 %copy-start.27 = (f32[1536]{0:T(1024)S(1)}, f32[1536]{0:T(1024)}, u32[]{:S(2)}) copy-start(f32[1536]{0:T(1024)} %param.16) | copy-start | bytes 18436
  330.6 72.2 %copy-start.1 = (bf16[384,1536]{1,0:T(8,128)(2,1)S(1)}, bf16[384,1536]{1,0:T(8,128)(2,1)}, u32[]{:S(2)}) copy-start(bf16[384,1536]{1,0:T(8,128)(2,1)} %param.13) | copy-start | bytes 3538948
  (6 other events, 8.0 us)
Sparse Core Ops, SparseCore 0:
  11.7 33.8 reduce-scatter.2
  48.9 38.7 all-gather.1
  330.7 69.7 reduce-scatter.4
where the time goes:
time: 411 us; the launch traced here: 409 us
  waiting for transfers between devices  241 us (59%)
  local copies, waits for them, and re-layouts  72 us (18%)
  other arithmetic  27 us (7%)
  matrix products  23.6 us (6%)
  starting transfers between devices  17 us (4%)
  blocking collectives  14.7 us (4%)
  between operations  14.4 us (4%)
    reduce_scatter x1, waiting for transfers between devices, on_device(): lax.psum_scatter(partial.reshape(n_exp * tok_rows, model_width), 'expert'...  69.9 us
    all_to_all x1, waiting for transfers between devices, on_device(): y_recv = lax.all_to_all(y_send, 'dp', 0, 0, tiled=True)  64.7 us
    all_to_all x1, waiting for transfers between devices, on_device(): lax.all_to_all(jnp.stack(weight_parts), 'dp', 0, 0, tiled=True)  57.2 us
    all_to_all x1, waiting for transfers between devices, on_device(): x_recv = lax.all_to_all(jnp.stack(x_parts), 'dp', 0, 0, tiled=True)  45.9 us
    another operation x18, local copies, waits for them, and re-layouts, as_rows(): return piece.reshape(-1, lane_width)  20.5 us
    unnamed x83, local copies, waits for them, and re-layouts  15.6 us
    all_gather x1, blocking collectives, on_device(): lax.all_gather(jnp.concatenate([expert_ids, replica_pick], axis=1), 'expe...  14.7 us
    slice x3, local copies, waits for them, and re-layouts, take(): piece = weight_recv[:, offset:offset + count].reshape((n_dp,) + shape)  8.72 us
  transfers between devices with their start and end apart: 6, of which 6 were waited for; matrix products, arithmetic and copies ran while one was open for 21% of the time, Pallas kernels for 0%

commit v1 on v0

--- a/solution.py
+++ b/solution.py
@@ -178,7 +178,20 @@
                 [slot_in[:, s] for s in owned_full[o]] + [slot_in[:, s] for s, _ in owned_part[o]]
             )
         )
-    x_recv = lax.all_to_all(jnp.stack(x_parts), "dp", 0, 0, tiled=True)
+    x = jnp.stack(x_parts)
+    ways, here_2 = (lax.axis_size("dp"), lax.axis_index("dp"))
+    width_2 = x.shape[0] // ways
+    lengths = list(x.shape)
+    lengths[0] = width_2
+    height = lengths[0]
+    lengths[0] = height * ways
+    full_2 = jnp.zeros(lengths, x.dtype)
+    for mask in range(ways):
+        part_2 = lax.dynamic_slice_in_dim(x, (here_2 ^ mask) * width_2, width_2, axis=0)
+        if mask:
+            part_2 = lax.ppermute(part_2, "dp", [(d, d ^ mask) for d in range(ways)])
+        full_2 = lax.dynamic_update_slice_in_dim(full_2, part_2, (here_2 ^ mask) * height, axis=0)
+    x_recv = full_2
     unit_rows = n_dp * n_exp * CAP_MOST
 
     def expert_rows(rows, w_up, w_down, width):

time: 411 us -> 426 us (1.036)
  local copies, waits for them, and re-layouts: 72 us -> 85.4 us
  waiting for transfers between devices: 241 us -> 250 us
  other arithmetic: 27 us -> 22.1 us
    all_to_all x1 -> x0, waiting for transfers between devices: 45.9 us -> none  [on_device(): x_recv = lax.all_to_all(jnp.stack(x_parts), 'dp', 0, 0, tiled=True)]
    ppermute x0 -> x3, waiting for transfers between devices: none -> 36.6 us  [on_device(): part_2 = lax.ppermute(part_2, 'dp', [(d, d ^ mask) for d in range(ways)])]
    reduce_scatter x1, waiting for transfers between devices: 2.73 us -> 27.1 us  [on_device(): lax.psum_scatter(jnp.dot(flat_context, w_proj, preferred_element_type=jnp...]
    dynamic_update_slice x0 -> x3, local copies, waits for them, and re-layouts: none -> 8.1 us  [on_device(): lax.dynamic_update_slice_in_dim(full_2, part_2, (here_2 ^ mask) * height,...]
    unnamed x83 -> x99, local copies, waits for them, and re-layouts: 15.6 us -> 9.76 us
    all_to_all x1 -> x0, starting transfers between devices: 5.54 us -> none  [on_device(): x_recv = lax.all_to_all(jnp.stack(x_parts), 'dp', 0, 0, tiled=True)]
    all_to_all x1, waiting for transfers between devices: 57.2 us -> 52.1 us  [on_device(): lax.all_to_all(jnp.stack(weight_parts), 'dp', 0, 0, tiled=True)]
  transfers between devices with their start and end apart: 6 -> 8, of which waited for: 6 -> 6; matrix products, arithmetic and copies ran while one was open for 21% -> 21% of each run, Pallas kernels for 0% -> 0%
where the time goes in v1:
time: 426 us; the launch traced here: 425 us
  waiting for transfers between devices  250 us (59%)
  local copies, waits for them, and re-layouts  85.4 us (20%)
  matrix products  23.8 us (6%)
  other arithmetic  22.1 us (5%)
  starting transfers between devices  15 us (4%)
  between operations  14.4 us (3%)
  blocking collectives  14.2 us (3%)
    reduce_scatter x1, waiting for transfers between devices, on_device(): lax.psum_scatter(partial.reshape(n_exp * tok_rows, model_width), 'expert'...  69.9 us
    all_to_all x1, waiting for transfers between devices, on_device(): y_recv = lax.all_to_all(y_send, 'dp', 0, 0, tiled=True)  64.5 us
    all_to_all x1, waiting for transfers between devices, on_device(): lax.all_to_all(jnp.stack(weight_parts), 'dp', 0, 0, tiled=True)  52.1 us
    ppermute x3, waiting for transfers between devices, on_device(): part_2 = lax.ppermute(part_2, 'dp', [(d, d ^ mask) for d in range(ways)])  36.6 us
    reduce_scatter x1, waiting for transfers between devices, on_device(): lax.psum_scatter(jnp.dot(flat_context, w_proj, preferred_element_type=jnp...  27.1 us
    another operation x18, local copies, waits for them, and re-layouts, as_rows(): return piece.reshape(-1, lane_width)  23.2 us
    all_gather x1, blocking collectives, on_device(): lax.all_gather(jnp.concatenate([expert_ids, replica_pick], axis=1), 'expe...  14.2 us
    unnamed x99, local copies, waits for them, and re-layouts  9.76 us
  transfers between devices with their start and end apart: 8, of which 6 were waited for; matrix products, arithmetic and copies ran while one was open for 21% of the time, Pallas kernels for 0%

profile of v1, /device:TPU:0, one launch (start us, length us, event | category | flops | bytes accessed | tf_op | source)
XLA Modules:
  0.0 425.0 jit_solution(10567164242771093573)
XLA Ops:
  8.4 3.3 convolution_convert_fusion.3
  13.3 3.2 fusion.61
  16.6 2.1 reshape_squeeze.63
  18.7 27.1 %reduce-scatter.3.cloned.1.call-done = bf16[128,1536]{1,0:T(8,128)(2,1)} async-done(((bf16[512,1536]{1,0:T(8,128)(2,1)}), bf16[128,1536]{1,0:T(8,128)(2,1)}) %reduce-scatter.3.cloned.1.call-update) | async-done | bytes 393232 | tf_op jit(solution)/shard_map/reduce_scatter | solution.py:142
  49.0 2.7 fusion.60
  76.2 3.7 pad_maximum_fusion
  79.9 5.7 %all-to-all-start = ((bf16[4,1920,512]{2,1,0:T(8,128)(2,1)}), bf16[4,1920,512]{2,1,0:T(8,128)(2,1)}, u32[]{:S(2)}, u32[]{:S(2)}) async-start(bf16[4,1920,512]{2,1,0:T(8,128)(2,1)} %pad_maximum_fusion), calls=%async_computation.1 | async-start | bytes 15728640 | tf_op jit(solution)/shard_map/all_to_all | solution.py:117
  85.7 14.2 %all_gather.6 = s32[1024,16]{0,1:T(8,128)S(1)} all-gather(s32[128,16]{0,1:T(8,128)S(1)} %pad_add_fusion), channel_id=1, replica_groups=mesh['dp'=4,'expert'=8] {'expert'}, dimensions={0}, use_global_device_ids=true | all-gather | bytes 73728 | tf_op jit(solution)/shard_map/all_gather | solution.py:138
  106.7 3.3 convolution_convert_fusion
  112.1 3.4 broadcast_in_dim.91
  115.5 2.7 constant_dynamic-slice_fusion
  118.2 2.0 collective-permute-start
  121.7 52.1 %all-to-all-done = bf16[4,1920,512]{2,1,0:T(8,128)(2,1)} async-done(((bf16[4,1920,512]{2,1,0:T(8,128)(2,1)}), bf16[4,1920,512]{2,1,0:T(8,128)(2,1)}, u32[]{:S(2)}, u32[]{:S(2)}) %all-to-all-start) | async-done | bytes 7864352 | tf_op jit(solution)/shard_map/all_to_all | solution.py:117
  173.7 3.8 slice.193
  177.6 5.6 %reshape_reshape.6 = bf16[1536,1024]{1,0:T(8,128)(2,1)} reshape(bf16[4,768,512]{2,1,0:T(8,128)(2,1)} %slice.193) | data formatting | bytes 6291456 | tf_op jit(solution)/shard_map/reshape;reshape | solution.py:129
  183.2 3.4 fusion.57
  186.6 3.7 reshape_reshape.7
  190.3 2.4 fusion.58
  192.6 2.1 concatenate.29
  198.7 8.7 %collective-permute-done = bf16[1,2,8,32,1536]{4,3,2,1,0:T(8,128)(2,1)} collective-permute-done((bf16[1,2,8,32,1536]{4,3,2,1,0:T(8,128)(2,1)}, bf16[1,2,8,32,1536]{4,3,2,1,0:T(8,128)(2,1)}, u32[]{:S(2)}, u32[]{:S(2)}) %collective-permute-start) | collective-permute-done | bytes 1572896 | tf_op jit(solution)/shard_map/ppermute | solution.py:192
  207.4 2.7 constant_dynamic-update-slice_fusion.22
  210.2 2.7 constant_dynamic-update-slice_fusion.21
  212.8 27.9 %collective-permute-done.2 = bf16[1,2,8,32,1536]{4,3,2,1,0:T(8,128)(2,1)} collective-permute-done((bf16[1,2,8,32,1536]{4,3,2,1,0:T(8,128)(2,1)}, bf16[1,2,8,32,1536]{4,3,2,1,0:T(8,128)(2,1)}, u32[]{:S(2)}, u32[]{:S(2)}) %collective-permute-start.2) | collective-permute-done | bytes 1572896 | tf_op jit(solution)/shard_map/ppermute | solution.py:192
  240.8 2.7 constant_dynamic-update-slice_fusion.20
  243.5 3.4 fusion.59
  247.2 3.4 fusion.64
  255.3 3.2 maximum_bitcast_fusion
  258.5 5.4 %all-to-all-start.1 = ((bf16[4,2,8,32,1536]{4,3,2,1,0:T(8,128)(2,1)}), bf16[4,2,8,32,1536]{4,3,2,1,0:T(8,128)(2,1)}, u32[]{:S(2)}, u32[]{:S(2)}) async-start(bf16[4,2,8,32,1536]{4,3,2,1,0:T(8,128)(2,1)} %maximum_bitcast_fusion), calls=%async_computation.2 | async-start | bytes 12582912 | tf_op jit(solution)/shard_map/all_to_all | solution.py:218
  264.2 2.9 convolution_bitcast_fusion
  268.6 64.5 %all-to-all-done.1 = bf16[4,2,8,32,1536]{4,3,2,1,0:T(8,128)(2,1)} async-done(((bf16[4,2,8,32,1536]{4,3,2,1,0:T(8,128)(2,1)}), bf16[4,2,8,32,1536]{4,3,2,1,0:T(8,128)(2,1)}, u32[]{:S(2)}, u32[]{:S(2)}) %all-to-all-start.1) | async-done | bytes 6291488 | tf_op jit(solution)/shard_map/all_to_all | solution.py:218
  342.5 3.7 convolution_add_fusion
  346.3 69.9 %reduce-scatter.5.cloned.1.call-done = f32[128,1536]{1,0:T(8,128)} async-done(((f32[1024,1536]{1,0:T(8,128)}), f32[128,1536]{1,0:T(8,128)}) %reduce-scatter.5.cloned.1.call-update) | async-done | bytes 786448 | tf_op jit(solution)/shard_map/reduce_scatter | solution.py:237
  (174 shorter events, 63.0 us)
Async XLA Ops:
  7.2 38.6 %reduce-scatter.3.cloned.1.call-start = ((), (), s32[]{:S(2)}) async-start(), calls=%async_computation.4 | async-start | bytes 1966080 | tf_op jit(solution)/shard_map/reduce_scatter | solution.py:142
  8.4 3.4 copy-start.9
  11.8 94.9 %all-gather.2.cloned.1.call-start = ((), (), s32[]{:S(2)}) async-start(), calls=%async_computation.5 | async-start | bytes 3538944 | tf_op jit(solution)/shard_map/all_gather | solution.py:152
  13.3 32.5 %copy-start.2 = (bf16[128,1536]{1,0:T(8,128)(2,1)S(1)}, bf16[128,1536]{1,0:T(8,128)(2,1)}, u32[]{:S(2)}) copy-start(bf16[128,1536]{1,0:T(8,128)(2,1)} %param.14) | copy-start | bytes 1179652
  16.6 30.4 %copy-start.34 = (f32[1536]{0:T(1024)S(1)}, f32[1536]{0:T(1024)}, u32[]{:S(2)}) copy-start(f32[1536]{0:T(1024)} %param.15) | copy-start | bytes 18436
  48.9 4.4 %copy-start.14 = (bf16[1,128,1536]{2,1,0:T(8,128)(2,1)S(1)}, bf16[1,128,1536]{2,1,0:T(8,128)(2,1)}, u32[]{:S(2)}) copy-start(bf16[1,128,1536]{2,1,0:T(8,128)(2,1)} %get-tuple-element.36) | copy-start | bytes 1179652
  54.3 8.2 %copy-start.13 = (bf16[1,128,1536]{2,1,0:T(8,128)(2,1)S(1)}, bf16[1,128,1536]{2,1,0:T(8,128)(2,1)}, u32[]{:S(2)}) copy-start(bf16[1,128,1536]{2,1,0:T(8,128)(2,1)} %get-tuple-element.35) | copy-start | bytes 1179652
  58.8 7.5 %copy-start.12 = (bf16[1,128,1536]{2,1,0:T(8,128)(2,1)S(1)}, bf16[1,128,1536]{2,1,0:T(8,128)(2,1)}, u32[]{:S(2)}) copy-start(bf16[1,128,1536]{2,1,0:T(8,128)(2,1)} %get-tuple-element.38) | copy-start | bytes 1179652
  63.4 5.0 %copy-start.22 = (bf16[1,384,256]{2,1,0:T(8,128)(2,1)S(1)}, bf16[1,384,256]{2,1,0:T(8,128)(2,1)}, u32[]{:S(2)}) copy-start(bf16[1,384,256]{2,1,0:T(8,128)(2,1)} %get-tuple-element.29) | copy-start | bytes 589828
  64.6 4.6 %copy-start.21 = (bf16[1,384,256]{2,1,0:T(8,128)(2,1)S(1)}, bf16[1,384,256]{2,1,0:T(8,128)(2,1)}, u32[]{:S(2)}) copy-start(bf16[1,384,256]{2,1,0:T(8,128)(2,1)} %get-tuple-element.23) | copy-start | bytes 589828
  64.6 7.1 %copy-start.11 = (bf16[1,128,1536]{2,1,0:T(8,128)(2,1)S(1)}, bf16[1,128,1536]{2,1,0:T(8,128)(2,1)}, u32[]{:S(2)}) copy-start(bf16[1,128,1536]{2,1,0:T(8,128)(2,1)} %get-tuple-element.39) | copy-start | bytes 1179652
  67.2 5.4 %copy-start.5 = (bf16[768,512]{1,0:T(8,128)(2,1)S(1)}, bf16[768,512]{1,0:T(8,128)(2,1)}, u32[]{:S(2)}) copy-start(bf16[768,512]{1,0:T(8,128)(2,1)} %reshape_squeeze.63) | copy-start | bytes 2359300
  69.1 3.6 copy-start.26
  69.9 2.9 copy-start.6
  79.9 5.7 %copy-start.37 = (s32[128,8]{0,1:T(8,128)S(1)}, s32[128,8]{0,1:T(8,128)}, u32[]{:S(2)}) copy-start(s32[128,8]{0,1:T(8,128)} %param.19) | copy-start | bytes 12292
  79.9 5.7 %copy-start.38 = (s32[128,8]{0,1:T(8,128)S(1)}, s32[128,8]{0,1:T(8,128)}, u32[]{:S(2)}) copy-start(s32[128,8]{0,1:T(8,128)} %param.18) | copy-start | bytes 12292
  79.9 20.3 %copy-start.36 = (s32[48]{0:T(128)S(1)}, s32[48]{0:T(128)}, u32[]{:S(2)}) copy-start(s32[48]{0:T(128)} %param.20) | copy-start | bytes 580
  79.9 93.8 %all-to-all-start = ((bf16[4,1920,512]{2,1,0:T(8,128)(2,1)}), bf16[4,1920,512]{2,1,0:T(8,128)(2,1)}, u32[]{:S(2)}, u32[]{:S(2)}) async-start(bf16[4,1920,512]{2,1,0:T(8,128)(2,1)} %pad_maximum_fusion), calls=%async_computation.1 | async-start | bytes 15728640 | tf_op jit(solution)/shard_map/all_to_all | solution.py:117
  102.1 2.7 copy-start.39
  118.2 89.2 %collective-permute-start = (bf16[1,2,8,32,1536]{4,3,2,1,0:T(8,128)(2,1)}, bf16[1,2,8,32,1536]{4,3,2,1,0:T(8,128)(2,1)}, u32[]{:S(2)}, u32[]{:S(2)}) collective-permute-start(bf16[1,2,8,32,1536]{4,3,2,1,0:T(8,128)(2,1)} %get-tuple-element.14), channel_id=1, source_target_pairs={{0,8},{8,0},{16,24},{24,16},{1,9},{9,1},{17,25},{25,17},{2,10},{10... | collective-permute-start | bytes 4718600 | tf_op jit(solution)/shard_map/ppermute | solution.py:192
  120.2 90.0 %collective-permute-start.1 = (bf16[1,2,8,32,1536]{4,3,2,1,0:T(8,128)(2,1)}, bf16[1,2,8,32,1536]{4,3,2,1,0:T(8,128)(2,1)}, u32[]{:S(2)}, u32[]{:S(2)}) collective-permute-start(bf16[1,2,8,32,1536]{4,3,2,1,0:T(8,128)(2,1)} %get-tuple-element.13), channel_id=1, source_target_pairs={{0,16},{8,24},{16,0},{24,8},{1,17},{9,25},{17,1},{25,9},{2,18},{10... | collective-permute-start | bytes 4718600 | tf_op jit(solution)/shard_map/ppermute | solution.py:192
  121.7 119.1 %collective-permute-start.2 = (bf16[1,2,8,32,1536]{4,3,2,1,0:T(8,128)(2,1)}, bf16[1,2,8,32,1536]{4,3,2,1,0:T(8,128)(2,1)}, u32[]{:S(2)}, u32[]{:S(2)}) collective-permute-start(bf16[1,2,8,32,1536]{4,3,2,1,0:T(8,128)(2,1)} %get-tuple-element.12), channel_id=1, source_target_pairs={{0,24},{8,16},{16,8},{24,0},{1,25},{9,17},{17,9},{25,1},{2,26},{10... | collective-permute-start | bytes 4718600 | tf_op jit(solution)/shard_map/ppermute | solution.py:192
  243.5 3.7 copy-start.4
  247.2 3.4 copy-start.10
  250.6 1.9 copy-start.23
  250.6 1.9 copy-start.24
  258.5 5.7 %copy-start.33 = (bf16[1536,40]{0,1:T(8,128)(2,1)S(1)}, bf16[1536,40]{0,1:T(8,128)(2,1)}, u32[]{:S(2)}) copy-start(bf16[1536,40]{0,1:T(8,128)(2,1)} %param.17) | copy-start | bytes 368644
  258.5 74.5 %all-to-all-start.1 = ((bf16[4,2,8,32,1536]{4,3,2,1,0:T(8,128)(2,1)}), bf16[4,2,8,32,1536]{4,3,2,1,0:T(8,128)(2,1)}, u32[]{:S(2)}, u32[]{:S(2)}) async-start(bf16[4,2,8,32,1536]{4,3,2,1,0:T(8,128)(2,1)} %maximum_bitcast_fusion), calls=%async_computation.2 | async-start | bytes 12582912 | tf_op jit(solution)/shard_map/all_to_all | solution.py:218
  263.9 152.3 %reduce-scatter.5.cloned.1.call-start = ((), (), s32[]{:S(2)}) async-start(), calls=%async_computation.6 | async-start | bytes 7077888 | tf_op jit(solution)/shard_map/reduce_scatter | solution.py:237
  346.2 69.9 %copy-start.3 = (bf16[128,1536]{1,0:T(8,128)(2,1)S(1)}, bf16[128,1536]{1,0:T(8,128)(2,1)}, u32[]{:S(2)}) copy-start(bf16[128,1536]{1,0:T(8,128)(2,1)} %reduce-scatter.3.cloned.1.call-done) | copy-start | bytes 1179652
  346.3 71.3 %copy-start.35 = (f32[1536]{0:T(1024)S(1)}, f32[1536]{0:T(1024)}, u32[]{:S(2)}) copy-start(f32[1536]{0:T(1024)} %param.16) | copy-start | bytes 18436
  346.3 72.2 %copy-start.1 = (bf16[384,1536]{1,0:T(8,128)(2,1)S(1)}, bf16[384,1536]{1,0:T(8,128)(2,1)}, u32[]{:S(2)}) copy-start(bf16[384,1536]{1,0:T(8,128)(2,1)} %param.13) | copy-start | bytes 3538948
  (16 other events, 17.8 us)
Sparse Core Ops, SparseCore 0:
  11.9 33.8 reduce-scatter.2
  49.1 38.1 all-gather.1
  346.4 69.7 reduce-scatter.4
